TPU v7x, 512 devices: a whole 4x8x8 slice. The times are simulated.
512 devices in a mesh: seq: 32 (over x_lo, z, core), tensor: 16 (over x_hi, y).
Axes of the slice: x: 4 (x_hi: 2, x_lo: 2; x = x_hi * 2 + x_lo), y: 8, z: 8, core: 2. Of those that a mesh axis runs over, the one named last changes fastest.
Arguments:
- qkv: bfloat16 [3, 8192, 8192], P(None, 'seq', 'tensor'), may hold values from -6 to 6
- conv_weight: float32 [3, 3, 8192], P(None, None, 'tensor'), may hold values from -3.6 to 3.6
- decay_rate: float32 [16, 8192], P(None, 'tensor'), may hold values from 1e-05 to 0.06
- residue: float32 [16, 8192], P(None, 'tensor'), may hold values from -3 to 3
- skip_gain: float32 [8192], P('tensor'), may hold values from -5 to 5
- out_weight: bfloat16 [8192, 8192], P('seq', 'tensor'), may hold values from -0.125 to 0.125
Outputs:
- mixer_out: bfloat16 [8192, 8192], P('seq', 'tensor')
All inputs are finite; a program needn't handle non-finite values.
Results may differ from a plain program's by a relative error of at most 0.0049.
Values may be sent and summed in bfloat16 or wider, within the bound.
No kernel may reach another device: no remote copies, remote signals or barrier semaphores. Data moves between devices by JAX's collectives and lax.ppermute only.
A program may use at most 64 MiB of HBM per device.

v0:
```python
from functools import partial
import jax
import jax.numpy as jnp
from jax import lax
from jax.sharding import PartitionSpec as P

KS = 3
PRECISE = lax.Precision.HIGHEST


def passed_along(block, axis, distance):
    devices = range(lax.axis_size(axis))
    route = [(i - distance, i) for i in devices if i - distance in devices]
    return lax.ppermute(block, axis, route)


def prefix_2(part, axis, combine, identity):
    place = lax.axis_index(axis)
    gathered = jax.tree.map(lambda a: lax.all_gather(a, axis), part)
    state = jax.tree.map(lambda a, e: jnp.zeros_like(a) + jnp.asarray(e, a.dtype), part, identity)

    def one(step, state):
        return combine(
            state, jax.tree.map(lambda a: lax.dynamic_index_in_dim(a, step, 0, False), gathered)
        )

    return lax.fori_loop(0, place, one, state)


def mode_tables(rate_block, residue_block, length):
    lag_values = jnp.arange(length, dtype=jnp.float32)
    decay_table = jnp.exp(-rate_block[:, None, :] * lag_values[None, :, None])
    mode_weight = residue_block * jnp.sqrt(-jnp.expm1(-2.0 * rate_block))
    return (decay_table, mode_weight)


def toeplitz(filter_taps):
    length = filter_taps.shape[0]
    lag_index = jnp.arange(length)[:, None] - jnp.arange(length)[None, :]
    picked = filter_taps[jnp.maximum(lag_index, 0), :]
    return jnp.where(lag_index[:, :, None] >= 0, picked, 0.0)


def inner_block(block_len, inputs):
    x_block, rate_block, residue_block = inputs
    decay_table, mode_weight = mode_tables(rate_block, residue_block, block_len)
    filter_taps = jnp.einsum("mc,mdc->dc", mode_weight, decay_table, precision=PRECISE)
    inner_part = jnp.einsum("tsc,nsc->ntc", toeplitz(filter_taps), x_block, precision=PRECISE)
    local_state = jnp.einsum("msc,nsc->nmc", decay_table[:, ::-1, :], x_block, precision=PRECISE)
    block_decay = jnp.exp(-rate_block * block_len)

    def advance(state, segment):
        return (state * block_decay + segment, state)

    section_state, entering = lax.scan(
        advance, jnp.zeros(rate_block.shape, jnp.float32), local_state
    )
    return (inner_part, entering, section_state)


def carry_block(block_len, inputs):
    rate_block, residue_block, block_entering, section_entering = inputs
    decay_table, mode_weight = mode_tables(rate_block, residue_block, block_len)
    block_ids = jnp.arange(block_entering.shape[0], dtype=jnp.float32)
    reach_back = jnp.exp(-rate_block[None] * (block_len * block_ids)[:, None, None])
    entering_all = block_entering + reach_back * section_entering[None]
    later_table = decay_table * jnp.exp(-rate_block)[:, None, :]
    return jnp.einsum("mc,mdc,nmc->ndc", mode_weight, later_table, entering_all, precision=PRECISE)


def combine_modes(earlier, later):
    return (earlier[0] * later[0], earlier[1] * later[0] + later[1])


def local(qkv, conv_weight, decay_rate, residue, skip_gain, out_weight):
    tokens_here = qkv.shape[1]
    channels = qkv.shape[2]
    modes = decay_rate.shape[0]
    tail_rows = qkv[:, tokens_here - (KS - 1) :, :]
    previous = passed_along(tail_rows, "seq", 1)
    extended = jnp.concatenate([previous, qkv], axis=1).astype(jnp.float32)
    filtered = jnp.zeros((3, tokens_here, channels), jnp.float32)
    for offset in range(KS):
        start_row = KS - 1 - offset
        filtered = (
            filtered
            + conv_weight[:, offset, None, :] * extended[:, start_row : start_row + tokens_here, :]
        )
    product = filtered[1] * filtered[2]
    group_width = min(channels, 128)
    groups = channels // group_width
    block_len = min(tokens_here, 64)
    block_count = tokens_here // block_len
    x_groups = product.reshape(block_count, block_len, groups, group_width).transpose(2, 0, 1, 3)
    rate_groups = decay_rate.reshape(modes, groups, group_width).transpose(1, 0, 2)
    residue_groups = residue.reshape(modes, groups, group_width).transpose(1, 0, 2)
    inner_part, block_entering, section_state = lax.map(
        partial(inner_block, block_len), (x_groups, rate_groups, residue_groups)
    )
    section_state = section_state.transpose(1, 0, 2).reshape(modes, channels)
    section_decay = jnp.exp(-decay_rate * tokens_here)
    identity = (
        jnp.ones(section_state.shape, jnp.float32),
        jnp.zeros(section_state.shape, jnp.float32),
    )
    prefix = prefix_2((section_decay, section_state), "seq", combine_modes, identity)
    section_entering = prefix[1].reshape(modes, groups, group_width).transpose(1, 0, 2)
    carried = lax.map(
        partial(carry_block, block_len),
        (rate_groups, residue_groups, block_entering, section_entering),
    )
    long_part = (inner_part + carried).transpose(1, 2, 0, 3).reshape(tokens_here, channels)
    long_part = long_part + skip_gain[None, :] * product
    mixed_local = (filtered[0] * long_part).astype(jnp.bfloat16)
    features = lax.all_gather(mixed_local, "tensor", axis=1, tiled=True)
    projected = jnp.dot(
        features,
        lax.all_gather(out_weight, "seq", axis=0, tiled=True),
        preferred_element_type=jnp.float32,
    )
    return projected.astype(jnp.bfloat16)


def solution(mesh):
    return jax.shard_map(
        local,
        mesh=mesh,
        in_specs=(
            P(None, "seq", "tensor"),
            P(None, None, "tensor"),
            P(None, "tensor"),
            P(None, "tensor"),
            P("tensor"),
            P("seq", "tensor"),
        ),
        out_specs=P("seq", "tensor"),
        check_vma=False,
    )
```

profile of v0, /device:TPU:1, one launch (start us, length us, event | category | flops | bytes accessed | tf_op | source)
XLA Modules:
  0.0 445.3 jit_solution(3757608169586370454)
XLA Ops:
  7.4 5.4 %collective-permute-start = (bf16[3,2,512]{2,1,0:T(2,128)(2,1)S(1)}, bf16[3,2,512]{2,1,0:T(2,128)(2,1)S(1)}, u32[]{:S(2)}, u32[]{:S(2)}) collective-permute-start(bf16[3,2,512]{2,1,0:T(2,128)(2,1)S(1)} %slice.31), channel_id=1, source_target_pairs={{0,16},{16,32},{32,48},{48,64},{64,80},{80,96},{96,112},{112,128},... | collective-permute-start | bytes 18440 | tf_op jit(solution)/shard_map/ppermute | solution.py:14
  12.7 1.4 multiply_exponential_fusion.2
  16.1 0.9 copy.35
  17.9 1.2 copy-done
  19.3 1.1 broadcast.65.clone
  20.4 119.2 %while.50 = (s32[]{:T(128)}, f32[4,4,64,128]{2,1,3,0:T(4,128)}, f32[4,4,16,128]{3,2,1,0:T(8,128)}, f32[4,16,128]{2,1,0:T(8,128)}, f32[4,4,64,128]{3,0,2,1:T(4,12...) while((s32[]{:T(128)}, f32[4,4,64,128]{2,1,3,0:T(4,128)}, ...), condition=%wide.region_3.4_spmd, body=%wide.region_0.3_spmd.sunk | while | flops 32536580 | bytes 16271129 | solution.py:97
  21.7 1.8 convolution_bitcast_fusion.3
  25.9 10.8 %gather_fusion = f32[4096,128]{1,0:T(8,128)S(1)} fusion(f32[64,128]{1,0:T(8,128)S(1)} %bitcast.132, s32[4096]{0:T(1024)S(1)} %broadcast_clamp_fusion.2), kind=kCustom, calls=%fused_computation.clone.1 | custom fusion | bytes 4210688 | tf_op jit(solution)/shard_map/while/body/eval_jaxpr/gather | solution.py:40
  36.7 4.5 %copy.70 = f32[64,64,128]{1,0,2:T(8,128)} copy(f32[64,64,128]{2,1,0:T(8,128)S(1)} %bitcast.133) | data formatting | bytes 4194304 | tf_op jit(solution)/shard_map/while/body/eval_jaxpr/gather | solution.py:40
  41.2 9.0 %fusion.52 = f32[4,4,64,128]{2,1,3,0:T(4,128)} fusion(f32[4,4,64,128]{2,1,3,0:T(4,128)} %get-tuple-element.485, s32[]{:T(128)} %get-tuple-element.484, f32[64,64,128]{1,0,2:T(8,128)} %copy.70, pred[64,64]{1,0:T(8,128)(4,1)S(1)} %subtract_compare_fusion.2, f32[1,4,64,128]{2,1,3,0:T(4,128)S(1)} %copy.71), kind=kOutput, calls=%fused_computation.32.clone.1 | convolution fusion | flops 25690112 | bytes 4592128 | tf_op jit(solution)/shard_map/while/body/eval_jaxpr/tsc,nsc->ntc/dot_general | solution.py:48
  51.5 1.8 convolution_bitcast_fusion.3
  55.7 10.8 %gather_fusion = f32[4096,128]{1,0:T(8,128)S(1)} fusion(f32[64,128]{1,0:T(8,128)S(1)} %bitcast.132, s32[4096]{0:T(1024)S(1)} %broadcast_clamp_fusion.2), kind=kCustom, calls=%fused_computation.clone.1 | custom fusion | bytes 4210688 | tf_op jit(solution)/shard_map/while/body/eval_jaxpr/gather | solution.py:40
  66.5 4.5 %copy.70 = f32[64,64,128]{1,0,2:T(8,128)} copy(f32[64,64,128]{2,1,0:T(8,128)S(1)} %bitcast.133) | data formatting | bytes 4194304 | tf_op jit(solution)/shard_map/while/body/eval_jaxpr/gather | solution.py:40
  71.0 9.0 %fusion.52 = f32[4,4,64,128]{2,1,3,0:T(4,128)} fusion(f32[4,4,64,128]{2,1,3,0:T(4,128)} %get-tuple-element.485, s32[]{:T(128)} %get-tuple-element.484, f32[64,64,128]{1,0,2:T(8,128)} %copy.70, pred[64,64]{1,0:T(8,128)(4,1)S(1)} %subtract_compare_fusion.2, f32[1,4,64,128]{2,1,3,0:T(4,128)S(1)} %copy.71), kind=kOutput, calls=%fused_computation.32.clone.1 | convolution fusion | flops 25690112 | bytes 4592128 | tf_op jit(solution)/shard_map/while/body/eval_jaxpr/tsc,nsc->ntc/dot_general | solution.py:48
  81.3 1.8 convolution_bitcast_fusion.3
  85.5 10.8 %gather_fusion = f32[4096,128]{1,0:T(8,128)S(1)} fusion(f32[64,128]{1,0:T(8,128)S(1)} %bitcast.132, s32[4096]{0:T(1024)S(1)} %broadcast_clamp_fusion.2), kind=kCustom, calls=%fused_computation.clone.1 | custom fusion | bytes 4210688 | tf_op jit(solution)/shard_map/while/body/eval_jaxpr/gather | solution.py:40
  96.3 4.5 %copy.70 = f32[64,64,128]{1,0,2:T(8,128)} copy(f32[64,64,128]{2,1,0:T(8,128)S(1)} %bitcast.133) | data formatting | bytes 4194304 | tf_op jit(solution)/shard_map/while/body/eval_jaxpr/gather | solution.py:40
  100.8 9.0 %fusion.52 = f32[4,4,64,128]{2,1,3,0:T(4,128)} fusion(f32[4,4,64,128]{2,1,3,0:T(4,128)} %get-tuple-element.485, s32[]{:T(128)} %get-tuple-element.484, f32[64,64,128]{1,0,2:T(8,128)} %copy.70, pred[64,64]{1,0:T(8,128)(4,1)S(1)} %subtract_compare_fusion.2, f32[1,4,64,128]{2,1,3,0:T(4,128)S(1)} %copy.71), kind=kOutput, calls=%fused_computation.32.clone.1 | convolution fusion | flops 25690112 | bytes 4592128 | tf_op jit(solution)/shard_map/while/body/eval_jaxpr/tsc,nsc->ntc/dot_general | solution.py:48
  111.1 1.8 convolution_bitcast_fusion.3
  115.3 10.8 %gather_fusion = f32[4096,128]{1,0:T(8,128)S(1)} fusion(f32[64,128]{1,0:T(8,128)S(1)} %bitcast.132, s32[4096]{0:T(1024)S(1)} %broadcast_clamp_fusion.2), kind=kCustom, calls=%fused_computation.clone.1 | custom fusion | bytes 4210688 | tf_op jit(solution)/shard_map/while/body/eval_jaxpr/gather | solution.py:40
  126.1 4.5 %copy.70 = f32[64,64,128]{1,0,2:T(8,128)} copy(f32[64,64,128]{2,1,0:T(8,128)S(1)} %bitcast.133) | data formatting | bytes 4194304 | tf_op jit(solution)/shard_map/while/body/eval_jaxpr/gather | solution.py:40
  130.6 9.0 %fusion.52 = f32[4,4,64,128]{2,1,3,0:T(4,128)} fusion(f32[4,4,64,128]{2,1,3,0:T(4,128)} %get-tuple-element.485, s32[]{:T(128)} %get-tuple-element.484, f32[64,64,128]{1,0,2:T(8,128)} %copy.70, pred[64,64]{1,0:T(8,128)(4,1)S(1)} %subtract_compare_fusion.2, f32[1,4,64,128]{2,1,3,0:T(4,128)S(1)} %copy.71), kind=kOutput, calls=%fused_computation.32.clone.1 | convolution fusion | flops 25690112 | bytes 4592128 | tf_op jit(solution)/shard_map/while/body/eval_jaxpr/tsc,nsc->ntc/dot_general | solution.py:48
  141.1 70.4 %all-gather.6.cloned.1.call-done = f32[32,16,512]{2,1,0:T(8,128)} async-done(((f32[1,16,512]{2,1,0:T(8,128)}), f32[32,16,512]{2,1,0:T(8,128)}) %all-gather.6.cloned.1.call-update) | async-done | bytes 1048592 | tf_op jit(solution)/shard_map/all_gather | solution.py:19
  212.6 11.1 %while.52 = (s32[]{:T(128)}, f32[4,4,64,128]{2,1,3,0:T(4,128)S(1)}, f32[4,4,16,128]{3,2,1,0:T(8,128)}, f32[4,16,128]{1,2,0:T(8,128)S(1)}, f32[4,16,128]{1,2,0:T(...) while((s32[]{:T(128)}, f32[4,4,64,128]{2,1,3,0:T(4,128)S(1)}, f32[4,4,16,128]{3,2,1,0:T(8,128)}, ...), condition=%wide.region_7.8_spmd, body=%wide.region_6.7_spmd.sunk | while | flops 6594566 | bytes 1049197 | solution.py:108
  213.7 1.7 fusion.56
  216.4 1.7 fusion.56
  219.2 1.7 fusion.56
  222.0 1.7 fusion.56
  225.4 0.9 fusion.32
  226.9 126.3 %all-gather.8.cloned.1.call-done = bf16[256,8192]{1,0:T(8,128)(2,1)} async-done(((bf16[256,512]{1,0:T(8,128)(2,1)}), bf16[256,8192]{1,0:T(8,128)(2,1)}) %all-gather.8.cloned.1.call-update) | async-done | bytes 4194320 | tf_op jit(solution)/shard_map/all_gather | solution.py:115
  353.2 77.9 %all-gather.10.cloned.1.call-done = bf16[8192,512]{1,0:T(8,128)(2,1)} async-done(((bf16[256,512]{1,0:T(8,128)(2,1)}), bf16[8192,512]{1,0:T(8,128)(2,1)}) %all-gather.10.cloned.1.call-update) | async-done | bytes 8388624 | tf_op jit(solution)/shard_map/all_gather | solution.py:118
  431.1 7.7 %convolution_convert_fusion = bf16[256,512]{1,0:T(8,128)(2,1)} fusion(bf16[256,8192]{1,0:T(8,128)(2,1)} %all-gather.8.cloned.1.call-done, bf16[8192,512]{1,0:T(8,128)(2,1)} %all-gather.10.cloned.1.call-done), kind=kOutput, calls=%fused_computation.53 | convolution fusion | flops 2147614720 | bytes 12845056 | tf_op jit(solution)/shard_map/dot_general | solution.py:116
  (174 shorter events, 28.5 us)
Async XLA Ops:
  6.5 10.6 %copy-start.3 = (bf16[3,256,512]{2,1,0:T(8,128)(2,1)S(1)}, bf16[3,256,512]{2,1,0:T(8,128)(2,1)}, u32[]{:S(2)}) copy-start(bf16[3,256,512]{2,1,0:T(8,128)(2,1)} %param.14) | copy-start | bytes 2359300
  6.5 134.6 %all-gather.12.cloned.1.call-start = ((), (), s32[]{:S(2)}) async-start(), calls=%async_computation.3 | async-start | bytes 1081344 | tf_op jit(solution)/shard_map/all_gather | solution.py:19
  7.4 9.8 %collective-permute-start = (bf16[3,2,512]{2,1,0:T(2,128)(2,1)S(1)}, bf16[3,2,512]{2,1,0:T(2,128)(2,1)S(1)}, u32[]{:S(2)}, u32[]{:S(2)}) collective-permute-start(bf16[3,2,512]{2,1,0:T(2,128)(2,1)S(1)} %slice.31), channel_id=1, source_target_pairs={{0,16},{16,32},{32,48},{48,64},{64,80},{80,96},{96,112},{112,128},... | collective-permute-start | bytes 18440 | tf_op jit(solution)/shard_map/ppermute | solution.py:14
  14.2 197.3 %all-gather.6.cloned.1.call-start = ((), (), s32[]{:S(2)}) async-start(), calls=%async_computation | async-start | bytes 1081344 | tf_op jit(solution)/shard_map/all_gather | solution.py:19
  17.8 1.2 copy-start
  141.0 212.1 %all-gather.8.cloned.1.call-start = ((), (), s32[]{:S(2)}) async-start(), calls=%async_computation.1 | async-start | bytes 4456448 | tf_op jit(solution)/shard_map/all_gather | solution.py:115
  212.6 11.1 %copy-start.2 = (f32[4,4,64,128]{2,1,3,0:T(4,128)S(1)}, f32[4,4,64,128]{2,1,3,0:T(4,128)}, u32[]{:S(2)}) copy-start(f32[4,4,64,128]{2,1,3,0:T(4,128)} %get-tuple-element.148) | copy-start | bytes 1572868
  224.0 1.4 copy-start.1
  224.0 1.4 copy-start.4
  226.3 204.8 %all-gather.10.cloned.1.call-start = ((), (), s32[]{:S(2)}) async-start(), calls=%async_computation.2 | async-start | bytes 8650752 | tf_op jit(solution)/shard_map/all_gather | solution.py:118
Sparse Core Ops, SparseCore 0:
  14.3 70.3 all-gather.11
  141.2 70.2 all-gather.5
  226.5 126.6 all-gather.7
  355.2 75.8 all-gather.9
where the time goes:
time: 448 us; the launch traced here: 445 us
  waiting for transfers between devices  275 us (61%)
  local copies, waits for them, and re-layouts  83.7 us (19%)
  matrix products  57.6 us (13%)
  between operations  13.3 us (3%)
  other arithmetic  9.04 us (2%)
  starting transfers between devices  5.51 us (1%)
    all_gather x1, waiting for transfers between devices, local(): features = lax.all_gather(mixed_local, 'tensor', axis=1, tiled=True)  126 us
    all_gather x1, waiting for transfers between devices, local(): lax.all_gather(out_weight, 'seq', axis=0, tiled=True)  77.9 us
    all_gather x2, waiting for transfers between devices, prefix_2(): gathered = jax.tree.map(lambda a: lax.all_gather(a, axis), part)  70.4 us
    gather x8, local copies, waits for them, and re-layouts, toeplitz(): picked = filter_taps[jnp.maximum(lag_index, 0), :]  61.1 us
    dot_general x4, matrix products, inner_block(): jnp.einsum('tsc,nsc->ntc', toeplitz(filter_taps), x_block, precision=PREC...  36 us
  transfers between devices with their start and end apart: 5, of which 3 were waited for; matrix products, arithmetic and copies ran while one was open for 28% of the time, Pallas kernels for 0%

commit v1 on v0

--- a/solution.py
+++ b/solution.py
@@ -112,7 +112,10 @@
     long_part = (inner_part + carried).transpose(1, 2, 0, 3).reshape(tokens_here, channels)
     long_part = long_part + skip_gain[None, :] * product
     mixed_local = (filtered[0] * long_part).astype(jnp.bfloat16)
-    features = lax.all_gather(mixed_local, "tensor", axis=1, tiled=True)
+    features = jnp.concatenate(
+        lax.all_to_all(jnp.stack([mixed_local] * lax.psum(1, "tensor"), axis=0), "tensor", 0, 0),
+        axis=1,
+    )
     projected = jnp.dot(
         features,
         lax.all_gather(out_weight, "seq", axis=0, tiled=True),

time: 448 us -> 365 us (0.81)
  the two profiles are of different devices: /device:TPU:1 before, /device:TPU:451 now
where the time goes in v1:
time: 365 us; the launch traced here: 362 us
  blocking collectives  104 us (28%)
  local copies, waits for them, and re-layouts  85.2 us (23%)
  waiting for transfers between devices  65.7 us (18%)
  matrix products  57.6 us (16%)
  other arithmetic  33 us (9%)
  between operations  13.3 us (4%)
    all_to_all x1, blocking collectives, local(): lax.all_to_all(jnp.stack([mixed_local] * lax.psum(1, 'tensor'), axis=0),...  104 us
    all_gather x2, waiting for transfers between devices, prefix_2(): gathered = jax.tree.map(lambda a: lax.all_gather(a, axis), part)  65 us
    gather x8, local copies, waits for them, and re-layouts, toeplitz(): picked = filter_taps[jnp.maximum(lag_index, 0), :]  61.2 us
    dot_general x4, matrix products, inner_block(): jnp.einsum('tsc,nsc->ntc', toeplitz(filter_taps), x_block, precision=PREC...  36 us
    add x31, other arithmetic, combine_modes(): return (earlier[0] * later[0], earlier[1] * later[0] + later[1])  24.5 us
    dot_general x1, matrix products, local(): jnp.dot(features, lax.all_gather(out_weight, 'seq', axis=0, tiled=True),...  7.71 us
  transfers between devices with their start and end apart: 4, of which 1 were waited for; matrix products, arithmetic and copies ran while one was open for 46% of the time, Pallas kernels for 0%

profile of v1, /device:TPU:451, one launch (start us, length us, event | category | flops | bytes accessed | tf_op | source)
XLA Modules:
  0.0 362.2 jit_solution(3287141227440573558)
XLA Ops:
  7.4 1.3 collective-permute-start
  8.7 1.4 multiply_exponential_fusion.2
  13.8 1.2 copy-done
  15.2 1.2 broadcast.70.clone
  16.4 119.3 %while.50 = (s32[]{:T(128)}, f32[4,4,64,128]{2,1,3,0:T(4,128)}, f32[4,4,16,128]{3,2,1,0:T(8,128)}, f32[4,16,128]{2,1,0:T(8,128)}, f32[4,4,64,128]{3,0,2,1:T(4,12...) while((s32[]{:T(128)}, f32[4,4,64,128]{2,1,3,0:T(4,128)}, ...), condition=%wide.region_3.4_spmd, body=%wide.region_0.3_spmd.sunk | while | flops 32536580 | bytes 16271129 | solution.py:97
  17.7 1.8 convolution_bitcast_fusion.3
  21.9 10.8 %gather_fusion = f32[4096,128]{1,0:T(8,128)S(1)} fusion(f32[64,128]{1,0:T(8,128)S(1)} %bitcast.125, s32[4096]{0:T(1024)S(1)} %broadcast_clamp_fusion.2), kind=kCustom, calls=%fused_computation.clone.1 | custom fusion | bytes 4210688 | tf_op jit(solution)/shard_map/while/body/eval_jaxpr/gather | solution.py:40
  32.7 4.5 %copy.72 = f32[64,64,128]{1,0,2:T(8,128)} copy(f32[64,64,128]{2,1,0:T(8,128)S(1)} %bitcast.126) | data formatting | bytes 4194304 | tf_op jit(solution)/shard_map/while/body/eval_jaxpr/gather | solution.py:40
  37.2 9.0 %fusion.51 = f32[4,4,64,128]{2,1,3,0:T(4,128)} fusion(f32[4,4,64,128]{2,1,3,0:T(4,128)} %get-tuple-element.485, s32[]{:T(128)} %get-tuple-element.484, f32[64,64,128]{1,0,2:T(8,128)} %copy.72, pred[64,64]{1,0:T(8,128)(4,1)S(1)} %subtract_compare_fusion.2, f32[1,4,64,128]{2,1,3,0:T(4,128)S(1)} %copy.73), kind=kOutput, calls=%fused_computation.32.clone.1 | convolution fusion | flops 25690112 | bytes 4592128 | tf_op jit(solution)/shard_map/while/body/eval_jaxpr/tsc,nsc->ntc/dot_general | solution.py:48
  47.5 1.8 convolution_bitcast_fusion.3
  51.7 10.8 %gather_fusion = f32[4096,128]{1,0:T(8,128)S(1)} fusion(f32[64,128]{1,0:T(8,128)S(1)} %bitcast.125, s32[4096]{0:T(1024)S(1)} %broadcast_clamp_fusion.2), kind=kCustom, calls=%fused_computation.clone.1 | custom fusion | bytes 4210688 | tf_op jit(solution)/shard_map/while/body/eval_jaxpr/gather | solution.py:40
  62.5 4.5 %copy.72 = f32[64,64,128]{1,0,2:T(8,128)} copy(f32[64,64,128]{2,1,0:T(8,128)S(1)} %bitcast.126) | data formatting | bytes 4194304 | tf_op jit(solution)/shard_map/while/body/eval_jaxpr/gather | solution.py:40
  67.0 9.0 %fusion.51 = f32[4,4,64,128]{2,1,3,0:T(4,128)} fusion(f32[4,4,64,128]{2,1,3,0:T(4,128)} %get-tuple-element.485, s32[]{:T(128)} %get-tuple-element.484, f32[64,64,128]{1,0,2:T(8,128)} %copy.72, pred[64,64]{1,0:T(8,128)(4,1)S(1)} %subtract_compare_fusion.2, f32[1,4,64,128]{2,1,3,0:T(4,128)S(1)} %copy.73), kind=kOutput, calls=%fused_computation.32.clone.1 | convolution fusion | flops 25690112 | bytes 4592128 | tf_op jit(solution)/shard_map/while/body/eval_jaxpr/tsc,nsc->ntc/dot_general | solution.py:48
  77.3 1.8 convolution_bitcast_fusion.3
  81.5 10.8 %gather_fusion = f32[4096,128]{1,0:T(8,128)S(1)} fusion(f32[64,128]{1,0:T(8,128)S(1)} %bitcast.125, s32[4096]{0:T(1024)S(1)} %broadcast_clamp_fusion.2), kind=kCustom, calls=%fused_computation.clone.1 | custom fusion | bytes 4210688 | tf_op jit(solution)/shard_map/while/body/eval_jaxpr/gather | solution.py:40
  92.3 4.5 %copy.72 = f32[64,64,128]{1,0,2:T(8,128)} copy(f32[64,64,128]{2,1,0:T(8,128)S(1)} %bitcast.126) | data formatting | bytes 4194304 | tf_op jit(solution)/shard_map/while/body/eval_jaxpr/gather | solution.py:40
  96.9 9.0 %fusion.51 = f32[4,4,64,128]{2,1,3,0:T(4,128)} fusion(f32[4,4,64,128]{2,1,3,0:T(4,128)} %get-tuple-element.485, s32[]{:T(128)} %get-tuple-element.484, f32[64,64,128]{1,0,2:T(8,128)} %copy.72, pred[64,64]{1,0:T(8,128)(4,1)S(1)} %subtract_compare_fusion.2, f32[1,4,64,128]{2,1,3,0:T(4,128)S(1)} %copy.73), kind=kOutput, calls=%fused_computation.32.clone.1 | convolution fusion | flops 25690112 | bytes 4592128 | tf_op jit(solution)/shard_map/while/body/eval_jaxpr/tsc,nsc->ntc/dot_general | solution.py:48
  107.1 1.8 convolution_bitcast_fusion.3
  111.4 10.8 %gather_fusion = f32[4096,128]{1,0:T(8,128)S(1)} fusion(f32[64,128]{1,0:T(8,128)S(1)} %bitcast.125, s32[4096]{0:T(1024)S(1)} %broadcast_clamp_fusion.2), kind=kCustom, calls=%fused_computation.clone.1 | custom fusion | bytes 4210688 | tf_op jit(solution)/shard_map/while/body/eval_jaxpr/gather | solution.py:40
  122.1 4.5 %copy.72 = f32[64,64,128]{1,0,2:T(8,128)} copy(f32[64,64,128]{2,1,0:T(8,128)S(1)} %bitcast.126) | data formatting | bytes 4194304 | tf_op jit(solution)/shard_map/while/body/eval_jaxpr/gather | solution.py:40
  126.7 9.0 %fusion.51 = f32[4,4,64,128]{2,1,3,0:T(4,128)} fusion(f32[4,4,64,128]{2,1,3,0:T(4,128)} %get-tuple-element.485, s32[]{:T(128)} %get-tuple-element.484, f32[64,64,128]{1,0,2:T(8,128)} %copy.72, pred[64,64]{1,0:T(8,128)(4,1)S(1)} %subtract_compare_fusion.2, f32[1,4,64,128]{2,1,3,0:T(4,128)S(1)} %copy.73), kind=kOutput, calls=%fused_computation.32.clone.1 | convolution fusion | flops 25690112 | bytes 4592128 | tf_op jit(solution)/shard_map/while/body/eval_jaxpr/tsc,nsc->ntc/dot_general | solution.py:48
  137.9 65.0 %all-gather.5.cloned.1.call-done = f32[32,16,512]{2,1,0:T(8,128)} async-done(((f32[1,16,512]{2,1,0:T(8,128)}), f32[32,16,512]{2,1,0:T(8,128)}) %all-gather.5.cloned.1.call-update) | async-done | bytes 1048592 | tf_op jit(solution)/shard_map/all_gather | solution.py:19
  202.8 25.3 %while.51 = (s32[]{:T(128)}, f32[16,512]{1,0:T(8,128)S(1)}, s32[]{:T(128)}, f32[32,16,512]{2,1,0:T(8,128)}, f32[32,16,512]{2,1,0:T(8,128)}, /*index=5*/s32[]{:T(128)}, s32[]{:T(128)}, s32[]{:T(128)}) while((s32[]{:T(128)}, f32[16,512]{1,0:T(8,128)S(1)}, s32[]{:T(128)}, f32[32,16,512]{2,1,0:T(8,128)}, f32[32,16,512]{2,1,0:T(8,128)}, ...), condition=%wide.region_5.6_spmd, body=%wide.region_4.5_spmd.sunk | while | flops 16389 | bytes 131195 | solution.py:27
  228.4 11.1 %while.52 = (s32[]{:T(128)}, f32[4,4,64,128]{2,1,3,0:T(4,128)S(1)}, f32[4,4,16,128]{3,2,1,0:T(8,128)}, f32[4,16,128]{1,2,0:T(8,128)S(1)}, f32[4,16,128]{1,2,0:T(...) while((s32[]{:T(128)}, f32[4,4,64,128]{2,1,3,0:T(4,128)S(1)}, f32[4,4,16,128]{3,2,1,0:T(8,128)}, ...), condition=%wide.region_7.8_spmd, body=%wide.region_6.7_spmd.sunk | while | flops 6594566 | bytes 1049197 | solution.py:108
  229.6 1.7 fusion.55
  232.3 1.7 fusion.55
  235.1 1.7 fusion.55
  237.9 1.7 fusion.55
  239.6 1.2 add_bitcast_fusion
  240.8 2.0 reshape.117
  243.8 104.1 %all_to_all.5 = bf16[16,256,512]{1,2,0:T(8,128)(2,1)} all-to-all(bf16[16,256,512]{1,2,0:T(8,128)(2,1)S(1)} %stack.5), channel_id=1, replica_groups=mesh['seq'=32,'tensor'=16] {'tensor'}, dimensions={0} | all-to-all | bytes 8388608 | tf_op jit(solution)/shard_map/all_to_all | solution.py:116
  348.0 7.7 %convolution_convert_fusion = bf16[256,512]{1,0:T(8,128)(2,1)} fusion(bf16[256,8192]{0,1:T(8,128)(2,1)} %bitcast.127, bf16[8192,512]{1,0:T(8,128)(2,1)} %all-gather.7.cloned.1.call-done), kind=kOutput, calls=%fused_computation.53 | convolution fusion | flops 2147614720 | bytes 12845056 | tf_op jit(solution)/shard_map/dot_general | solution.py:119
  (204 shorter events, 51.7 us)
Async XLA Ops:
  6.5 6.5 %copy-start.3 = (bf16[3,256,512]{2,1,0:T(8,128)(2,1)S(1)}, bf16[3,256,512]{2,1,0:T(8,128)(2,1)}, u32[]{:S(2)}) copy-start(bf16[3,256,512]{2,1,0:T(8,128)(2,1)} %param.14) | copy-start | bytes 2359300
  6.5 131.3 %all-gather.9.cloned.1.call-start = ((), (), s32[]{:S(2)}) async-start(), calls=%async_computation.3 | async-start | bytes 1081344 | tf_op jit(solution)/shard_map/all_gather | solution.py:19
  7.4 5.6 %collective-permute-start = (bf16[3,2,512]{2,1,0:T(2,128)(2,1)S(1)}, bf16[3,2,512]{2,1,0:T(2,128)(2,1)S(1)}, u32[]{:S(2)}, u32[]{:S(2)}) collective-permute-start(bf16[3,2,512]{2,1,0:T(2,128)(2,1)S(1)} %slice.31), channel_id=1, source_target_pairs={{0,16},{16,32},{32,48},{48,64},{64,80},{80,96},{96,112},{112,128},... | collective-permute-start | bytes 18440 | tf_op jit(solution)/shard_map/ppermute | solution.py:14
  10.1 192.8 %all-gather.5.cloned.1.call-start = ((), (), s32[]{:S(2)}) async-start(), calls=%async_computation.1 | async-start | bytes 1081344 | tf_op jit(solution)/shard_map/all_gather | solution.py:19
  13.7 1.2 copy-start
  137.1 210.8 %all-gather.7.cloned.1.call-start = ((), (), s32[]{:S(2)}) async-start(), calls=%async_computation.2 | async-start | bytes 8650752 | tf_op jit(solution)/shard_map/all_gather | solution.py:121
  228.4 11.1 %copy-start.2 = (f32[4,4,64,128]{2,1,3,0:T(4,128)S(1)}, f32[4,4,64,128]{2,1,3,0:T(4,128)}, u32[]{:S(2)}) copy-start(f32[4,4,64,128]{2,1,3,0:T(4,128)} %get-tuple-element.148) | copy-start | bytes 1572868
  240.8 2.2 copy-start.1
  240.8 2.2 copy-start.4
Sparse Core Ops, SparseCore 0:
  10.2 65.5 all-gather.8
  137.2 65.5 all-gather.4
  205.0 96.8 all-gather.6
